TPU v7x, 32 devices: a whole 2x2x4 slice. The times are simulated.
32 devices in a mesh: seq: 8 (over z, y), tp: 4 (over x, core).
Axes of the slice: x: 2, y: 2, z: 4, core: 2. Of those that a mesh axis runs over, the one named last changes fastest.
Arguments:
- new_query: bfloat16 [8, 3584], P('seq', 'tp'), may hold values from -360 to 360
- new_key: bfloat16 [8, 512], P('seq', 'tp'), may hold values from -6 to 6
- new_value: bfloat16 [8, 512], P('seq', 'tp'), may hold values from -6 to 6
- cache_keys: bfloat16 [8, 4096, 512], P('seq', None, 'tp'), may hold values from -6 to 6
- cache_values: bfloat16 [8, 4096, 512], P('seq', None, 'tp'), may hold values from -6 to 6
- cache_length: int32 [8], P('seq'), may hold values from 1 to 4096, 16384 in all
- dealing: int32 [8], replicated, may hold values from 0 to 7, each once
- out_weight: bfloat16 [3584, 3584], P('tp', 'seq'), may hold values from -0.09375 to 0.09375
- stretch_query: bfloat16 [3, 256, 3584], P(None, 'seq', 'tp'), may hold values from -360 to 360
- stretch_key: bfloat16 [3, 256, 512], P(None, 'seq', 'tp'), may hold values from -6 to 6
- stretch_value: bfloat16 [3, 256, 512], P(None, 'seq', 'tp'), may hold values from -6 to 6
- prior_keys: bfloat16 [3, 8192, 512], P(None, 'seq', 'tp'), may hold values from -6 to 6
- prior_values: bfloat16 [3, 8192, 512], P(None, 'seq', 'tp'), may hold values from -6 to 6
- stretch_start: int32 [3], replicated, may hold values from 1 to 8192, 16384 in all
Outputs:
- decode_mixed: bfloat16 [8, 3584], P('tp', 'seq')
- stretch_out: bfloat16 [3, 256, 3584], P(None, 'seq', 'tp')
Inputs may be any that keep to these rules, and one draw needn't show every extreme that they name: dealing[a] is the cache slot of the decode request that arrives a-th; every slot appears once. `cache_length`: cached positions in use of each decode slot; one slot is full. `stretch_start`: cached positions of each stretch's request that precede the stretch; one request's cache is full.
All inputs are finite; a program needn't handle non-finite values. No bound on the sum of `cache_length` on one device may be relied on, other than what follows from the above.
Results may differ from a plain program's by a relative error of at most 0.0051.
Values may be sent and summed in bfloat16 or wider, within the bound.
No kernel may reach another device: no remote copies, remote signals or barrier semaphores. Data moves between devices by JAX's collectives and lax.ppermute only.
A program may use at most 64 MiB of HBM per device.

v0:
```python
import math
import jax
import jax.numpy as jnp
from jax import lax
from jax.sharding import PartitionSpec as P

NEG_FILL = -1e30


def partial_attend(queries, keys, values, visible):
    factor = 1.0 / math.sqrt(queries.shape[-1])
    scores = jnp.dot(queries, keys.T, preferred_element_type=jnp.float32) * factor
    scores = jnp.where(visible, scores, NEG_FILL)
    row_top = jnp.max(scores, axis=1)
    weights = jnp.where(visible, jnp.exp(scores - row_top[:, None]), 0.0)
    weight_sum = jnp.sum(weights, axis=1)
    numerator = jnp.dot(weights.astype(jnp.bfloat16), values, preferred_element_type=jnp.float32)
    return (row_top, weight_sum, numerator)


def body(
    new_query,
    new_key,
    new_value,
    cache_keys,
    cache_values,
    cache_length,
    dealing,
    out_weight,
    stretch_query,
    stretch_key,
    stretch_value,
    prior_keys,
    prior_values,
    stretch_start,
):
    head_size = cache_keys.shape[2]
    group_size = new_query.shape[1] // head_size
    local_dec = new_query.shape[0]
    seq_rank = lax.axis_index("seq")
    seq_count = lax.axis_size("seq")
    total_dec = local_dec * seq_count
    every_query, every_key, every_value = (
        lax.all_gather(new_query, "seq", axis=0, tiled=True),
        lax.all_gather(new_key, "seq", axis=0, tiled=True),
        lax.all_gather(new_value, "seq", axis=0, tiled=True),
    )
    slot_ids = seq_rank * local_dec + jnp.arange(local_dec, dtype=jnp.int32)
    arrival_ids = jnp.arange(total_dec, dtype=jnp.int32)
    sources = jnp.sum(
        jnp.where(dealing[None, :] == slot_ids[:, None], arrival_ids[None, :], 0), axis=1
    )
    home_query = jnp.take(every_query, sources, axis=0)
    home_key = jnp.take(every_key, sources, axis=0)
    home_value = jnp.take(every_value, sources, axis=0)
    cache_span = cache_keys.shape[1]
    cache_pos = jnp.arange(cache_span, dtype=jnp.int32)

    def decode_slot(query_row, own_key, own_value, cached_keys, cached_values, length):
        key_all = jnp.concatenate([cached_keys, own_key[None, :]], axis=0)
        value_all = jnp.concatenate([cached_values, own_value[None, :]], axis=0)
        visible = jnp.concatenate([cache_pos < length, jnp.ones((1,), dtype=jnp.bool_)])
        visible = jnp.broadcast_to(visible[None, :], (group_size, cache_span + 1))
        row_top, weight_sum, numerator = partial_attend(
            query_row.reshape(group_size, head_size), key_all, value_all, visible
        )
        return (
            (numerator / weight_sum[:, None]).astype(jnp.bfloat16).reshape(group_size * head_size)
        )

    home_out = jax.vmap(decode_slot)(
        home_query, home_key, home_value, cache_keys, cache_values, cache_length
    )
    stored_terms = jnp.dot(
        lax.all_gather(home_out, "seq", axis=0, tiled=True),
        out_weight,
        preferred_element_type=jnp.float32,
    )
    arrival_terms = jnp.take(stored_terms, dealing, axis=0)
    decode_mixed = lax.psum_scatter(arrival_terms, "tp", scatter_dimension=0, tiled=True).astype(
        jnp.bfloat16
    )
    stretch_count, local_tok, _ = stretch_query.shape
    stretch_len = local_tok * seq_count
    prior_span = prior_keys.shape[1]
    row_count = stretch_len * group_size
    every_stretch_key, every_stretch_value = (
        lax.all_gather(stretch_key, "seq", axis=1, tiled=True),
        lax.all_gather(stretch_value, "seq", axis=1, tiled=True),
    )
    gathered_query = lax.all_gather(stretch_query, "seq", axis=1, tiled=True)
    prior_pos = seq_rank * prior_span + jnp.arange(prior_span, dtype=jnp.int32)
    peak_list, total_list, numer_list = ([], [], [])
    for stretch_index in range(stretch_count):
        queries_all = gathered_query[stretch_index].reshape(row_count, head_size)
        prior_visible = jnp.broadcast_to(
            (prior_pos < stretch_start[stretch_index])[None, :], (row_count, prior_span)
        )

        def work_part():
            return partial_attend(
                queries_all, prior_keys[stretch_index], prior_values[stretch_index], prior_visible
            )

        def skip_part():
            return (
                jnp.full((row_count,), NEG_FILL, jnp.float32),
                jnp.zeros((row_count,), jnp.float32),
                jnp.zeros((row_count, head_size), jnp.float32),
            )

        pieces = lax.cond(
            seq_rank * prior_span < stretch_start[stretch_index], work_part, skip_part
        )
        peak_list.append(pieces[0].reshape(stretch_len, group_size))
        total_list.append(pieces[1].reshape(stretch_len, group_size))
        numer_list.append(pieces[2].reshape(stretch_len, group_size, head_size))
    part_top = jnp.stack(peak_list)
    part_sum = jnp.stack(total_list)
    part_num = jnp.stack(numer_list)
    peak_all = lax.pmax(part_top, "seq")
    factor = jnp.exp(part_top - peak_all)
    got_sum, got_num = (
        lax.psum_scatter(part_sum * factor, "seq", scatter_dimension=1, tiled=True),
        lax.psum_scatter(part_num * factor[..., None], "seq", scatter_dimension=1, tiled=True),
    )
    got_top = lax.dynamic_slice_in_dim(peak_all, seq_rank * local_tok, local_tok, 1)
    local_rows = local_tok * group_size
    stretch_pos = jnp.arange(stretch_len, dtype=jnp.int32)
    own_token = seq_rank * local_tok + jnp.arange(local_rows, dtype=jnp.int32) // group_size
    causal = stretch_pos[None, :] <= own_token[:, None]
    self_tops, self_totals, self_numers = ([], [], [])
    for stretch_index in range(stretch_count):
        local_queries = stretch_query[stretch_index].reshape(local_rows, head_size)
        pieces = partial_attend(
            local_queries,
            every_stretch_key[stretch_index],
            every_stretch_value[stretch_index],
            causal,
        )
        self_tops.append(pieces[0].reshape(local_tok, group_size))
        self_totals.append(pieces[1].reshape(local_tok, group_size))
        self_numers.append(pieces[2].reshape(local_tok, group_size, head_size))
    self_top = jnp.stack(self_tops)
    final_top = jnp.maximum(got_top, self_top)
    first_factor = jnp.exp(got_top - final_top)
    second_factor = jnp.exp(self_top - final_top)
    got_sum = got_sum * first_factor + jnp.stack(self_totals) * second_factor
    got_num = got_num * first_factor[..., None] + jnp.stack(self_numers) * second_factor[..., None]
    stretch_out = (
        (got_num / got_sum[..., None])
        .astype(jnp.bfloat16)
        .reshape(stretch_count, local_tok, group_size * head_size)
    )
    return (decode_mixed, stretch_out)


def solution(mesh):
    return jax.shard_map(
        body,
        mesh=mesh,
        in_specs=(
            P("seq", "tp"),
            P("seq", "tp"),
            P("seq", "tp"),
            P("seq", None, "tp"),
            P("seq", None, "tp"),
            P("seq"),
            P(),
            P("tp", "seq"),
            P(None, "seq", "tp"),
            P(None, "seq", "tp"),
            P(None, "seq", "tp"),
            P(None, "seq", "tp"),
            P(None, "seq", "tp"),
            P(),
        ),
        out_specs=(P("tp", "seq"), P(None, "seq", "tp")),
        check_vma=False,
    )
```

profile of v0, /device:TPU:0, one launch (start us, length us, event | category | flops | bytes accessed | tf_op | source)
XLA Modules:
  0.0 355.2 jit_solution(8637244430150871322)
XLA Ops:
  11.4 43.9 %all-gather.6.cloned.1.call-done = bf16[3,256,896]{2,1,0:T(8,128)(2,1)} async-done(((bf16[3,32,896]{2,1,0:T(8,128)(2,1)}), bf16[3,256,896]{2,1,0:T(8,128)(2,1)}) %all-gather.6.cloned.1.call-update) | async-done | bytes 1376272 | tf_op jit(solution)/shard_map/all_gather | solution.py:91
  55.3 21.5 %conditional.3 = (f32[1,256,7,128]{3,1,2,0:T(8,128)S(1)}, f32[1,256,7]{1,2,0:T(8,128)S(1)}, f32[1,256,7]{1,2,0:T(8,128)S(1)}) conditional(s32[]{:T(128)} %convert_element_type.44, () %tuple.51, (bf16[3,1024,128]{2,1,0:T(8,128)(2,1)}, bf16[3,256,896]{2,1,0:T(8,128)(2,1)}, s32[1024]{0:T(1024)S(1)}, bf16[3,1024,128]{2,1,0:T(8,128)(2,1)}, s32[]{:T(128)}) %tuple.52), branch_computations={%region_4.6_spmd, %region_5.9_spmd} | conditional | flops 956036608 | bytes 33706012 | solution.py:112
  59.6 3.8 %fusion.2 = (f32[1792]{0:T(1024)S(1)}, bf16[1792,1024]{1,0:T(8,128)(2,1)}) fusion(f32[1792,1024]{1,0:T(8,128)S(1)} %get-tuple-element.123, f32[1792]{0:T(1024)S(1)} %get-tuple-element.122, pred[1024]{0:T(1024)(128)(4,1)S(1)} %broadcast_compare_fusion), kind=kLoop, calls=%fused_computation.5 | loop fusion | flops 11008256 | bytes 11025408 | tf_op jit(solution)/shard_map/cond/branch_1_fun/reduce_sum | solution.py:16
  63.5 6.4 %reshape.159 = bf16[256,7,1024]{2,1,0:T(8,128)(2,1)} reshape(bf16[1792,1024]{1,0:T(8,128)(2,1)} %get-tuple-element.121) | data formatting | bytes 7340032 | tf_op jit(solution)/shard_map/reshape.122
  69.9 6.3 %fusion.5 = f32[1,256,7,128]{3,1,2,0:T(8,128)S(1)} fusion(bf16[256,7,1024]{2,1,0:T(8,128)(2,1)} %reshape.159, bf16[3,1024,128]{2,1,0:T(8,128)(2,1)} %get-tuple-element.37), kind=kOutput, calls=%fused_computation.8 | convolution fusion | flops 469762048 | bytes 5373952 | tf_op jit(solution)/shard_map/cond/branch_1_fun/dot_general | solution.py:17
  77.4 21.5 %conditional.4 = (f32[1,256,7,128]{3,1,2,0:T(8,128)S(1)}, f32[1,256,7]{1,2,0:T(8,128)S(1)}, f32[1,256,7]{1,2,0:T(8,128)S(1)}) conditional(s32[]{:T(128)} %convert_element_type.45, () %tuple.53, (bf16[3,1024,128]{2,1,0:T(8,128)(2,1)}, bf16[3,256,896]{2,1,0:T(8,128)(2,1)}, s32[1024]{0:T(1024)S(1)}, bf16[3,1024,128]{2,1,0:T(8,128)(2,1)}, ...), branch_computations={%region_8.10_spmd, %region_9.13_spmd} | conditional | flops 956036608 | bytes 33706012 | solution.py:112
  79.6 2.2 fusion.13
  81.8 3.9 %fusion.15 = (f32[1792]{0:T(1024)S(1)}, bf16[1792,1024]{1,0:T(8,128)(2,1)}) fusion(f32[1792,1024]{1,0:T(8,128)S(1)} %get-tuple-element.127, f32[1792]{0:T(1024)S(1)} %get-tuple-element.126, pred[1024]{0:T(1024)(128)(4,1)S(1)} %broadcast_compare_fusion.1), kind=kLoop, calls=%fused_computation.19 | loop fusion | flops 11008256 | bytes 11025408 | tf_op jit(solution)/shard_map/cond/branch_1_fun/reduce_sum | solution.py:16
  85.6 6.4 %reshape.160 = bf16[256,7,1024]{2,1,0:T(8,128)(2,1)} reshape(bf16[1792,1024]{1,0:T(8,128)(2,1)} %get-tuple-element.125) | data formatting | bytes 7340032 | tf_op jit(solution)/shard_map/reshape.125
  92.1 6.3 %fusion.18 = f32[1,256,7,128]{3,1,2,0:T(8,128)S(1)} fusion(bf16[256,7,1024]{2,1,0:T(8,128)(2,1)} %reshape.160, bf16[3,1024,128]{2,1,0:T(8,128)(2,1)} %get-tuple-element.41), kind=kOutput, calls=%fused_computation.22 | convolution fusion | flops 469762048 | bytes 5373952 | tf_op jit(solution)/shard_map/cond/branch_1_fun/dot_general | solution.py:17
  99.6 23.7 %conditional.5 = (f32[1,256,7,128]{3,1,2,0:T(8,128)}, f32[1,256,7]{1,2,0:T(8,128)}, f32[1,256,7]{1,2,0:T(8,128)S(1)}) conditional(s32[]{:T(128)} %convert_element_type.46, () %tuple.55, (bf16[3,1024,128]{2,1,0:T(8,128)(2,1)}, bf16[3,256,896]{2,1,0:T(8,128)(2,1)}, s32[1024]{0:T(1024)S(1)}, bf16[3,1024,128]{2,1,0:T(8,128)(2,1)}, s32[]{:T(128)}) %tuple.56), branch_computations={%region_12.14_spmd, %region_13.17_spmd} | conditional | flops 956036608 | bytes 33710136 | solution.py:112
  102.4 2.2 fusion.26
  104.6 3.8 %fusion.28 = (f32[1792]{0:T(1024)S(1)}, bf16[1792,1024]{1,0:T(8,128)(2,1)}) fusion(f32[1792,1024]{1,0:T(8,128)S(1)} %get-tuple-element.131, f32[1792]{0:T(1024)S(1)} %get-tuple-element.130, pred[1024]{0:T(1024)(128)(4,1)S(1)} %copy-done.7), kind=kLoop, calls=%fused_computation.33 | loop fusion | flops 11008256 | bytes 11025408 | tf_op jit(solution)/shard_map/cond/branch_1_fun/reduce_sum | solution.py:16
  108.4 6.4 %reshape.161 = bf16[256,7,1024]{2,1,0:T(8,128)(2,1)} reshape(bf16[1792,1024]{1,0:T(8,128)(2,1)} %get-tuple-element.129) | data formatting | bytes 7340032 | tf_op jit(solution)/shard_map/reshape.128
  114.9 7.2 %fusion.31 = f32[1,256,7,128]{3,1,2,0:T(8,128)} fusion(bf16[256,7,1024]{2,1,0:T(8,128)(2,1)} %reshape.161, bf16[3,1024,128]{2,1,0:T(8,128)(2,1)} %get-tuple-element.45), kind=kOutput, calls=%fused_computation.36 | convolution fusion | flops 469762048 | bytes 5373952 | tf_op jit(solution)/shard_map/cond/branch_1_fun/dot_general | solution.py:17
  124.6 34.1 %pmax.7 = f32[3,256,7]{1,2,0:T(8,128)S(1)} all-reduce(f32[3,256,7]{1,2,0:T(8,128)} %constant_dynamic-update-slice_fusion), channel_id=1, replica_groups=mesh['seq'=8,'tp'=4] {'seq'}, use_global_device_ids=true, to_apply=%region_16.18 | all-reduce | flops 5376 | bytes 43008 | tf_op jit(solution)/shard_map/pmax | solution.py:121
  162.5 3.0 maximum_multiply_fusion
  165.9 30.6 %all_gather.26 = bf16[3,256,128]{2,1,0:T(8,128)(2,1)S(1)} all-gather(bf16[3,32,128]{2,1,0:T(8,128)(2,1)S(1)} %copy-done.5), channel_id=1, replica_groups=mesh['seq'=8,'tp'=4] {'seq'}, dimensions={1}, use_global_device_ids=true | all-gather | bytes 221184 | tf_op jit(solution)/shard_map/all_gather | solution.py:88
  201.6 16.2 %all-gather.1 = bf16[8,1,128]{2,1,0:T(2,128)(2,1)S(1)} all-gather(bf16[1,1,128]{2,1,0:T(2,128)(2,1)S(1)} %bitcast.128), channel_id=1, replica_groups=mesh['seq'=8,'tp'=4] {'seq'}, dimensions={0}, use_global_device_ids=true | all-gather | bytes 2304 | tf_op jit(solution)/shard_map/all_gather | solution.py:45
  218.5 18.1 %all-gather.2 = bf16[8,1,128]{2,1,0:T(2,128)(2,1)S(1)} all-gather(bf16[1,1,128]{2,1,0:T(2,128)(2,1)S(1)} %bitcast.129), channel_id=1, replica_groups=mesh['seq'=8,'tp'=4] {'seq'}, dimensions={0}, use_global_device_ids=true | all-gather | bytes 2304 | tf_op jit(solution)/shard_map/all_gather | solution.py:46
  236.6 30.7 %all-gather = bf16[8,1,896]{2,1,0:T(2,128)(2,1)S(1)} all-gather(bf16[1,1,896]{2,1,0:T(2,128)(2,1)S(1)} %bitcast.125), channel_id=1, replica_groups=mesh['seq'=8,'tp'=4] {'seq'}, dimensions={0}, use_global_device_ids=true | all-gather | bytes 16128 | tf_op jit(solution)/shard_map/all_gather | solution.py:44
  271.0 30.4 %all-gather.3 = bf16[8,1,896]{2,1,0:T(2,128)(2,1)S(1)} all-gather(bf16[1,1,896]{2,1,0:T(2,128)(2,1)S(1)} %reshape.252), channel_id=1, replica_groups=mesh['seq'=8,'tp'=4] {'seq'}, dimensions={0}, use_global_device_ids=true | all-gather | bytes 16128 | tf_op jit(solution)/shard_map/all_gather | solution.py:75
  303.7 10.1 %all-reduce = bf16[8,448]{1,0:T(8,128)(2,1)S(1)} all-reduce(f32[8,448]{1,0:T(8,128)S(1)} %broadcast_select_fusion), channel_id=2, replica_groups=mesh['seq'=8,'tp'=4] {'tp'}, use_global_device_ids=true, to_apply=%region_3.5.clone | all-reduce | flops 3584 | bytes 21504
  313.9 30.6 %all_gather.27 = bf16[3,256,128]{2,1,0:T(8,128)(2,1)S(1)} all-gather(bf16[3,32,128]{2,1,0:T(8,128)(2,1)S(1)} %copy-done.6), channel_id=1, replica_groups=mesh['seq'=8,'tp'=4] {'seq'}, dimensions={1}, use_global_device_ids=true | all-gather | bytes 221184 | tf_op jit(solution)/shard_map/all_gather | solution.py:89
  (114 shorter events, 32.8 us)
Async XLA Ops:
  7.2 294.3 %copy-start = (bf16[896,448]{0,1:T(8,128)(2,1)S(1)}, bf16[896,448]{0,1:T(8,128)(2,1)}, u32[]{:S(2)}) copy-start(bf16[896,448]{0,1:T(8,128)(2,1)} %param.29) | copy-start | bytes 2408452
  7.2 48.1 %all-gather.6.cloned.1.call-start = ((), (), s32[]{:S(2)}) async-start(), calls=%async_computation.2 | async-start | bytes 1548288 | tf_op jit(solution)/shard_map/all_gather | solution.py:91
  7.9 337.7 %reduce-scatter.7.cloned.1.call-start = ((), (), s32[]{:S(2)}) async-start(), calls=%async_computation.4 | async-start | bytes 147456
  76.8 0.6 copy-start.3
  98.9 0.6 copy-start.4
  98.9 0.6 copy-start.2
  102.3 2.2 copy-start.7
  162.4 3.2 copy-start.1
  162.4 184.2 %reduce-scatter.5.cloned.1.call-start = ((), (), s32[]{:S(2)}) async-start(), calls=%async_computation.3 | async-start | bytes 3096576 | tf_op jit(solution)/shard_map/reduce_scatter | solution.py:125
  162.4 3.4 copy-start.5
  165.5 33.5 %copy-start.11 = (s32[8]{0:T(128)S(1)}, s32[8]{0:T(128)}, u32[]{:S(2)}) copy-start(s32[8]{0:T(128)} %param.28) | copy-start | bytes 100
  165.5 36.1 %copy-start.9 = (bf16[1,128]{1,0:T(2,128)(2,1)S(1)}, bf16[1,128]{1,0:T(2,128)(2,1)}, u32[]{:S(2)}) copy-start(bf16[1,128]{1,0:T(2,128)(2,1)} %param.23) | copy-start | bytes 772
  165.5 53.0 %copy-start.10 = (bf16[1,128]{1,0:T(2,128)(2,1)S(1)}, bf16[1,128]{1,0:T(2,128)(2,1)}, u32[]{:S(2)}) copy-start(bf16[1,128]{1,0:T(2,128)(2,1)} %param.24) | copy-start | bytes 772
  165.5 71.1 %copy-start.8 = (bf16[1,896]{1,0:T(2,128)(2,1)S(1)}, bf16[1,896]{1,0:T(2,128)(2,1)}, u32[]{:S(2)}) copy-start(bf16[1,896]{1,0:T(2,128)(2,1)} %param.22) | copy-start | bytes 5380
  165.6 136.8 %copy-start.12 = (u32[32]{0:T(128)S(1)}, u32[32]{0:T(128)}, u32[]{:S(2)}) copy-start(u32[32]{0:T(128)} %constant.174) | copy-start | bytes 388
  165.7 148.2 %copy-start.6 = (bf16[3,32,128]{2,1,0:T(8,128)(2,1)S(1)}, bf16[3,32,128]{2,1,0:T(8,128)(2,1)}, u32[]{:S(2)}) copy-start(bf16[3,32,128]{2,1,0:T(8,128)(2,1)} %param.32) | copy-start | bytes 73732
Sparse Core Ops, SparseCore 0:
  10.2 45.0 all-gather.5
  162.5 58.1 reduce-scatter.6
  224.3 70.5 reduce-scatter.4
where the time goes:
time: 357 us; the launch traced here: 355 us
  blocking collectives  201 us (56%)
  waiting for transfers between devices  44.6 us (12%)
  local copies, waits for them, and re-layouts  37.3 us (10%)
  matrix products  31.3 us (9%)
  other arithmetic  21.5 us (6%)
  between operations  19.3 us (5%)
    all_gather x1, waiting for transfers between devices, body(): gathered_query = lax.all_gather(stretch_query, 'seq', axis=1, tiled=True)  43.9 us
    pmax x1, blocking collectives, body(): peak_all = lax.pmax(part_top, 'seq')  34.1 us
    all_gather x1, blocking collectives, body(): lax.all_gather(new_query, 'seq', axis=0, tiled=True)  30.7 us
    all_gather x1, blocking collectives, body(): lax.all_gather(stretch_key, 'seq', axis=1, tiled=True)  30.6 us
    all_gather x1, blocking collectives, body(): lax.all_gather(stretch_value, 'seq', axis=1, tiled=True)  30.6 us
    all_gather x1, blocking collectives, body(): lax.all_gather(home_out, 'seq', axis=0, tiled=True)  30.4 us
    dot_general x7, matrix products, partial_attend(): jnp.dot(weights.astype(jnp.bfloat16), values, preferred_element_type=jnp....  21.8 us
    another operation x6, local copies, waits for them, and re-layouts  19.5 us
  transfers between devices with their start and end apart: 3, of which 1 were waited for; matrix products, arithmetic and copies ran while one was open for 4% of the time, Pallas kernels for 0%

commit v1 on v0

--- a/solution.py
+++ b/solution.py
@@ -3,8 +3,21 @@
 import jax.numpy as jnp
 from jax import lax
 from jax.sharding import PartitionSpec as P
+from jax.lax import axis_index, axis_size, ppermute
 
 NEG_FILL = -1e30
+
+
+def view_seats_all_on_mesh(state):
+    num_devices = axis_size("seq")
+    raw_out = [(t - 1, t) for t in range(1, num_devices)] + [(num_devices - 1, 0)]
+    response = state
+    panels = [response]
+    for _ in range(num_devices - 1):
+        response = ppermute(response, "seq", raw_out)
+        panels += [response]
+    local_next = jnp.concatenate([*reversed(panels)], axis=1)
+    return jnp.roll(local_next, (axis_index("seq") + 1) * response.shape[1], axis=1)
 
 
 def partial_attend(queries, keys, values, visible):
@@ -88,7 +101,7 @@
         lax.all_gather(stretch_key, "seq", axis=1, tiled=True),
         lax.all_gather(stretch_value, "seq", axis=1, tiled=True),
     )
-    gathered_query = lax.all_gather(stretch_query, "seq", axis=1, tiled=True)
+    gathered_query = view_seats_all_on_mesh(stretch_query)
     prior_pos = seq_rank * prior_span + jnp.arange(prior_span, dtype=jnp.int32)
     peak_list, total_list, numer_list = ([], [], [])
     for stretch_index in range(stretch_count):

time: 357 us -> 374 us (1.048)
  waiting for transfers between devices: 44.6 us -> 54 us
    ppermute x0 -> x7, waiting for transfers between devices: none -> 53.9 us  [view_seats_all_on_mesh(): response = ppermute(response, 'seq', raw_out)]
    all_gather x1 -> x0, waiting for transfers between devices: 43.9 us -> none  [body(): gathered_query = lax.all_gather(stretch_query, 'seq', axis=1, tiled=True)]
  transfers between devices with their start and end apart: 3 -> 9, of which waited for: 1 -> 7; matrix products, arithmetic and copies ran while one was open for 4% -> 4% of each run, Pallas kernels for 0% -> 0%
where the time goes in v1:
time: 374 us; the launch traced here: 373 us
  blocking collectives  200 us (53%)
  waiting for transfers between devices  54 us (14%)
  local copies, waits for them, and re-layouts  40.8 us (11%)
  matrix products  31.1 us (8%)
  other arithmetic  23.6 us (6%)
  between operations  19.7 us (5%)
    ppermute x7, waiting for transfers between devices, view_seats_all_on_mesh(): response = ppermute(response, 'seq', raw_out)  53.9 us
    pmax x1, blocking collectives, body(): peak_all = lax.pmax(part_top, 'seq')  33.6 us
    all_gather x1, blocking collectives, body(): lax.all_gather(stretch_key, 'seq', axis=1, tiled=True)  30.7 us
    all_gather x1, blocking collectives, body(): lax.all_gather(stretch_value, 'seq', axis=1, tiled=True)  30.6 us
    all_gather x1, blocking collectives, body(): lax.all_gather(home_out, 'seq', axis=0, tiled=True)  30.5 us
    all_gather x1, blocking collectives, body(): lax.all_gather(new_query, 'seq', axis=0, tiled=True)  30.5 us
    dot_general x7, matrix products, partial_attend(): jnp.dot(weights.astype(jnp.bfloat16), values, preferred_element_type=jnp....  22.9 us
    another operation x6, local copies, waits for them, and re-layouts  19.5 us
  transfers between devices with their start and end apart: 9, of which 7 were waited for; matrix products, arithmetic and copies ran while one was open for 4% of the time, Pallas kernels for 0%

profile of v1, /device:TPU:0, one launch (start us, length us, event | category | flops | bytes accessed | tf_op | source)
XLA Modules:
  0.0 372.9 jit_solution(5981373588750178979)
XLA Ops:
  10.3 7.6 %collective-permute-done = bf16[3,32,896]{2,1,0:T(8,128)(2,1)S(1)} collective-permute-done((bf16[3,32,896]{2,1,0:T(8,128)(2,1)}, bf16[3,32,896]{2,1,0:T(8,128)(2,1)S(1)}, u32[]{:S(2)}, u32[]{:S(2)}) %collective-permute-start) | collective-permute-done | bytes 172064 | tf_op jit(solution)/shard_map/ppermute | solution.py:17
  17.9 8.3 %collective-permute-done.1 = bf16[3,32,896]{2,1,0:T(8,128)(2,1)S(1)} collective-permute-done((bf16[3,32,896]{2,1,0:T(8,128)(2,1)S(1)}, bf16[3,32,896]{2,1,0:T(8,128)(2,1)S(1)}, u32[]{:S(2)}, u32[]{:S(2)}) %collective-permute-start.1) | collective-permute-done | bytes 172064 | tf_op jit(solution)/shard_map/ppermute | solution.py:17
  26.1 8.1 %collective-permute-done.2 = bf16[3,32,896]{2,1,0:T(8,128)(2,1)S(1)} collective-permute-done((bf16[3,32,896]{2,1,0:T(8,128)(2,1)S(1)}, bf16[3,32,896]{2,1,0:T(8,128)(2,1)S(1)}, u32[]{:S(2)}, u32[]{:S(2)}) %collective-permute-start.2) | collective-permute-done | bytes 172064 | tf_op jit(solution)/shard_map/ppermute | solution.py:17
  34.2 8.1 %collective-permute-done.3 = bf16[3,32,896]{2,1,0:T(8,128)(2,1)S(1)} collective-permute-done((bf16[3,32,896]{2,1,0:T(8,128)(2,1)S(1)}, bf16[3,32,896]{2,1,0:T(8,128)(2,1)S(1)}, u32[]{:S(2)}, u32[]{:S(2)}) %collective-permute-start.3) | collective-permute-done | bytes 172064 | tf_op jit(solution)/shard_map/ppermute | solution.py:17
  42.4 8.1 %collective-permute-done.4 = bf16[3,32,896]{2,1,0:T(8,128)(2,1)S(1)} collective-permute-done((bf16[3,32,896]{2,1,0:T(8,128)(2,1)S(1)}, bf16[3,32,896]{2,1,0:T(8,128)(2,1)S(1)}, u32[]{:S(2)}, u32[]{:S(2)}) %collective-permute-start.4) | collective-permute-done | bytes 172064 | tf_op jit(solution)/shard_map/ppermute | solution.py:17
  50.5 9.1 %collective-permute-done.5 = bf16[3,32,896]{2,1,0:T(8,128)(2,1)S(1)} collective-permute-done((bf16[3,32,896]{2,1,0:T(8,128)(2,1)S(1)}, bf16[3,32,896]{2,1,0:T(8,128)(2,1)S(1)}, u32[]{:S(2)}, u32[]{:S(2)}) %collective-permute-start.5) | collective-permute-done | bytes 172064 | tf_op jit(solution)/shard_map/ppermute | solution.py:17
  63.0 4.7 %collective-permute-done.6 = bf16[3,32,896]{2,1,0:T(8,128)(2,1)S(1)} collective-permute-done((bf16[3,32,896]{2,1,0:T(8,128)(2,1)S(1)}, bf16[3,32,896]{2,1,0:T(8,128)(2,1)S(1)}, u32[]{:S(2)}, u32[]{:S(2)}) %collective-permute-start.6) | collective-permute-done | bytes 172064 | tf_op jit(solution)/shard_map/ppermute | solution.py:17
  69.1 21.8 %conditional.3 = (f32[1,256,7,128]{3,1,2,0:T(8,128)S(1)}, f32[1,256,7]{1,2,0:T(8,128)}, f32[1,256,7]{1,2,0:T(8,128)}) conditional(s32[]{:T(128)} %convert_element_type.44, () %tuple.51, (bf16[3,1024,128]{2,1,0:T(8,128)(2,1)}, bf16[3,256,896]{2,1,0:T(8,128)(2,1)S(1)}, s32[1024]{0:T(1024)S(1)}, bf16[3,1024,128]{2,1,0:T(8,128)(2,1)}, s32[]{:T(128)}) %tuple.52), branch_computations={%region_4.6_spmd, %region_5.9_spmd} | conditional | flops 956036608 | bytes 33763412 | solution.py:125
  76.4 6.4 %reshape.159 = bf16[256,7,1024]{2,1,0:T(8,128)(2,1)} reshape(bf16[1792,1024]{1,0:T(8,128)(2,1)} %get-tuple-element.121) | data formatting | bytes 7340032 | tf_op jit(solution)/shard_map/reshape.122
  82.8 6.3 %fusion.5 = f32[1,256,7,128]{3,1,2,0:T(8,128)S(1)} fusion(bf16[256,7,1024]{2,1,0:T(8,128)(2,1)} %reshape.159, bf16[3,1024,128]{2,1,0:T(8,128)(2,1)} %get-tuple-element.37), kind=kOutput, calls=%fused_computation.8 | convolution fusion | flops 469762048 | bytes 5373952 | tf_op jit(solution)/shard_map/cond/branch_1_fun/dot_general | solution.py:30
  92.2 25.8 %conditional.4 = (f32[1,256,7,128]{3,1,2,0:T(8,128)}, f32[1,256,7]{1,2,0:T(8,128)}, f32[1,256,7]{1,2,0:T(8,128)}) conditional(s32[]{:T(128)} %convert_element_type.45, () %tuple.53, (bf16[3,1024,128]{2,1,0:T(8,128)(2,1)}, bf16[3,256,896]{2,1,0:T(8,128)(2,1)S(1)}, s32[1024]{0:T(1024)}, bf16[3,1024,128]{2,1,0:T(8,128)(2,1)}, s32[]{:T(128)}) %tuple.113), branch_computations={%region_8.10_spmd, %region_9.13_spmd} | conditional | flops 956036608 | bytes 33767536 | solution.py:125
  102.5 6.4 %reshape.160 = bf16[256,7,1024]{2,1,0:T(8,128)(2,1)} reshape(bf16[1792,1024]{1,0:T(8,128)(2,1)} %get-tuple-element.125) | data formatting | bytes 7340032 | tf_op jit(solution)/shard_map/reshape.125
  109.0 7.3 %fusion.18 = f32[1,256,7,128]{3,1,2,0:T(8,128)} fusion(bf16[256,7,1024]{2,1,0:T(8,128)(2,1)} %reshape.160, bf16[3,1024,128]{2,1,0:T(8,128)(2,1)} %get-tuple-element.41), kind=kOutput, calls=%fused_computation.22 | convolution fusion | flops 469762048 | bytes 5373952 | tf_op jit(solution)/shard_map/cond/branch_1_fun/dot_general | solution.py:30
  119.3 23.9 %conditional.5 = (f32[1,256,7,128]{3,1,2,0:T(8,128)}, f32[1,256,7]{1,2,0:T(8,128)}, f32[1,256,7]{1,2,0:T(8,128)}) conditional(s32[]{:T(128)} %convert_element_type.46, () %tuple.55, (bf16[3,1024,128]{2,1,0:T(8,128)(2,1)}, bf16[3,256,896]{2,1,0:T(8,128)(2,1)S(1)}, s32[1024]{0:T(1024)}, bf16[3,1024,128]{2,1,0:T(8,128)(2,1)}, s32[]{:T(128)}) %tuple.114), branch_computations={%region_12.14_spmd, %region_13.17_spmd} | conditional | flops 956036608 | bytes 33710136 | solution.py:125
  127.8 6.4 %reshape.161 = bf16[256,7,1024]{2,1,0:T(8,128)(2,1)} reshape(bf16[1792,1024]{1,0:T(8,128)(2,1)} %get-tuple-element.129) | data formatting | bytes 7340032 | tf_op jit(solution)/shard_map/reshape.128
  134.2 7.2 %fusion.31 = f32[1,256,7,128]{3,1,2,0:T(8,128)} fusion(bf16[256,7,1024]{2,1,0:T(8,128)(2,1)} %reshape.161, bf16[3,1024,128]{2,1,0:T(8,128)(2,1)} %get-tuple-element.45), kind=kOutput, calls=%fused_computation.36 | convolution fusion | flops 469762048 | bytes 5373952 | tf_op jit(solution)/shard_map/cond/branch_1_fun/dot_general | solution.py:30
  144.5 33.6 %pmax.7 = f32[3,256,7]{1,2,0:T(8,128)S(1)} all-reduce(f32[3,256,7]{1,2,0:T(8,128)} %constant_dynamic-update-slice_fusion.16), channel_id=1, replica_groups=mesh['seq'=8,'tp'=4] {'seq'}, use_global_device_ids=true, to_apply=%region_16.18 | all-reduce | flops 5376 | bytes 43008 | tf_op jit(solution)/shard_map/pmax | solution.py:134
  184.6 30.7 %all_gather.22 = bf16[3,256,128]{2,1,0:T(8,128)(2,1)S(1)} all-gather(bf16[3,32,128]{2,1,0:T(8,128)(2,1)S(1)} %copy-done.8), channel_id=1, replica_groups=mesh['seq'=8,'tp'=4] {'seq'}, dimensions={1}, use_global_device_ids=true | all-gather | bytes 221184 | tf_op jit(solution)/shard_map/all_gather | solution.py:101
  220.4 16.2 %all-gather.1 = bf16[8,1,128]{2,1,0:T(2,128)(2,1)S(1)} all-gather(bf16[1,1,128]{2,1,0:T(2,128)(2,1)S(1)} %bitcast.128), channel_id=1, replica_groups=mesh['seq'=8,'tp'=4] {'seq'}, dimensions={0}, use_global_device_ids=true | all-gather | bytes 2304 | tf_op jit(solution)/shard_map/all_gather | solution.py:58
  237.2 18.2 %all-gather.2 = bf16[8,1,128]{2,1,0:T(2,128)(2,1)S(1)} all-gather(bf16[1,1,128]{2,1,0:T(2,128)(2,1)S(1)} %bitcast.129), channel_id=1, replica_groups=mesh['seq'=8,'tp'=4] {'seq'}, dimensions={0}, use_global_device_ids=true | all-gather | bytes 2304 | tf_op jit(solution)/shard_map/all_gather | solution.py:59
  255.4 30.5 %all-gather = bf16[8,1,896]{2,1,0:T(2,128)(2,1)S(1)} all-gather(bf16[1,1,896]{2,1,0:T(2,128)(2,1)S(1)} %bitcast.125), channel_id=1, replica_groups=mesh['seq'=8,'tp'=4] {'seq'}, dimensions={0}, use_global_device_ids=true | all-gather | bytes 16128 | tf_op jit(solution)/shard_map/all_gather | solution.py:57
  288.4 30.5 %all-gather.3 = bf16[8,1,896]{2,1,0:T(2,128)(2,1)S(1)} all-gather(bf16[1,1,896]{2,1,0:T(2,128)(2,1)S(1)} %reshape.252), channel_id=1, replica_groups=mesh['seq'=8,'tp'=4] {'seq'}, dimensions={0}, use_global_device_ids=true | all-gather | bytes 16128 | tf_op jit(solution)/shard_map/all_gather | solution.py:88
  321.2 10.1 %all-reduce = bf16[8,448]{1,0:T(8,128)(2,1)S(1)} all-reduce(f32[8,448]{1,0:T(8,128)S(1)} %broadcast_select_fusion), channel_id=2, replica_groups=mesh['seq'=8,'tp'=4] {'tp'}, use_global_device_ids=true, to_apply=%region_3.5.clone | all-reduce | flops 3584 | bytes 21504
  331.3 30.6 %all_gather.23 = bf16[3,256,128]{2,1,0:T(8,128)(2,1)S(1)} all-gather(bf16[3,32,128]{2,1,0:T(8,128)(2,1)S(1)} %copy-done.9), channel_id=1, replica_groups=mesh['seq'=8,'tp'=4] {'seq'}, dimensions={1}, use_global_device_ids=true | all-gather | bytes 221184 | tf_op jit(solution)/shard_map/all_gather | solution.py:102
  (152 shorter events, 58.5 us)
Async XLA Ops:
  7.2 311.7 %copy-start = (bf16[896,448]{0,1:T(8,128)(2,1)S(1)}, bf16[896,448]{0,1:T(8,128)(2,1)}, u32[]{:S(2)}) copy-start(bf16[896,448]{0,1:T(8,128)(2,1)} %param.29) | copy-start | bytes 2408452
  7.2 61.8 %copy-start.1 = (bf16[3,32,896]{2,1,0:T(8,128)(2,1)S(1)}, bf16[3,32,896]{2,1,0:T(8,128)(2,1)}, u32[]{:S(2)}) copy-start(bf16[3,32,896]{2,1,0:T(8,128)(2,1)} %param.30) | copy-start | bytes 516100
  7.2 355.8 %reduce-scatter.7.cloned.1.call-start = ((), (), s32[]{:S(2)}) async-start(), calls=%async_computation.3 | async-start | bytes 147456
  7.2 10.6 %collective-permute-start = (bf16[3,32,896]{2,1,0:T(8,128)(2,1)}, bf16[3,32,896]{2,1,0:T(8,128)(2,1)S(1)}, u32[]{:S(2)}, u32[]{:S(2)}) collective-permute-start(bf16[3,32,896]{2,1,0:T(8,128)(2,1)} %param.30), channel_id=1, source_target_pairs={{0,4},{4,8},{8,12},{12,16},{16,20},{20,24},{24,28},{28,0},{1,5},{5... | collective-permute-start | bytes 516104 | tf_op jit(solution)/shard_map/ppermute | solution.py:17
  17.9 8.3 %collective-permute-start.1 = (bf16[3,32,896]{2,1,0:T(8,128)(2,1)S(1)}, bf16[3,32,896]{2,1,0:T(8,128)(2,1)S(1)}, u32[]{:S(2)}, u32[]{:S(2)}) collective-permute-start(bf16[3,32,896]{2,1,0:T(8,128)(2,1)S(1)} %collective-permute-done), channel_id=1, source_target_pairs={{0,4},{4,8},{8,12},{12,16},{16,20},{20,24},{24,28},{28,0},{1,5},{5... | collective-permute-start | bytes 516104 | tf_op jit(solution)/shard_map/ppermute | solution.py:17
  26.1 8.1 %collective-permute-start.2 = (bf16[3,32,896]{2,1,0:T(8,128)(2,1)S(1)}, bf16[3,32,896]{2,1,0:T(8,128)(2,1)S(1)}, u32[]{:S(2)}, u32[]{:S(2)}) collective-permute-start(bf16[3,32,896]{2,1,0:T(8,128)(2,1)S(1)} %collective-permute-done.1), channel_id=1, source_target_pairs={{0,4},{4,8},{8,12},{12,16},{16,20},{20,24},{24,28},{28,0},{1,5},{5... | collective-permute-start | bytes 516104 | tf_op jit(solution)/shard_map/ppermute | solution.py:17
  34.2 8.1 %collective-permute-start.3 = (bf16[3,32,896]{2,1,0:T(8,128)(2,1)S(1)}, bf16[3,32,896]{2,1,0:T(8,128)(2,1)S(1)}, u32[]{:S(2)}, u32[]{:S(2)}) collective-permute-start(bf16[3,32,896]{2,1,0:T(8,128)(2,1)S(1)} %collective-permute-done.2), channel_id=1, source_target_pairs={{0,4},{4,8},{8,12},{12,16},{16,20},{20,24},{24,28},{28,0},{1,5},{5... | collective-permute-start | bytes 516104 | tf_op jit(solution)/shard_map/ppermute | solution.py:17
  42.3 8.1 %collective-permute-start.4 = (bf16[3,32,896]{2,1,0:T(8,128)(2,1)S(1)}, bf16[3,32,896]{2,1,0:T(8,128)(2,1)S(1)}, u32[]{:S(2)}, u32[]{:S(2)}) collective-permute-start(bf16[3,32,896]{2,1,0:T(8,128)(2,1)S(1)} %collective-permute-done.3), channel_id=1, source_target_pairs={{0,4},{4,8},{8,12},{12,16},{16,20},{20,24},{24,28},{28,0},{1,5},{5... | collective-permute-start | bytes 516104 | tf_op jit(solution)/shard_map/ppermute | solution.py:17
  50.5 9.1 %collective-permute-start.5 = (bf16[3,32,896]{2,1,0:T(8,128)(2,1)S(1)}, bf16[3,32,896]{2,1,0:T(8,128)(2,1)S(1)}, u32[]{:S(2)}, u32[]{:S(2)}) collective-permute-start(bf16[3,32,896]{2,1,0:T(8,128)(2,1)S(1)} %collective-permute-done.4), channel_id=1, source_target_pairs={{0,4},{4,8},{8,12},{12,16},{16,20},{20,24},{24,28},{28,0},{1,5},{5... | collective-permute-start | bytes 516104 | tf_op jit(solution)/shard_map/ppermute | solution.py:17
  59.5 8.1 %collective-permute-start.6 = (bf16[3,32,896]{2,1,0:T(8,128)(2,1)S(1)}, bf16[3,32,896]{2,1,0:T(8,128)(2,1)S(1)}, u32[]{:S(2)}, u32[]{:S(2)}) collective-permute-start(bf16[3,32,896]{2,1,0:T(8,128)(2,1)S(1)} %collective-permute-done.5), channel_id=1, source_target_pairs={{0,4},{4,8},{8,12},{12,16},{16,20},{20,24},{24,28},{28,0},{1,5},{5... | collective-permute-start | bytes 516104 | tf_op jit(solution)/shard_map/ppermute | solution.py:17
  63.0 6.2 %copy-start.7 = (s32[1024]{0:T(1024)}, s32[1024]{0:T(1024)S(1)}, u32[]{:S(2)}) copy-start(s32[1024]{0:T(1024)S(1)} %iota_add_fusion) | copy-start | bytes 12292
  72.5 3.9 %copy-start.3 = (f32[1792]{0:T(1024)}, f32[1792]{0:T(1024)S(1)}, u32[]{:S(2)}) copy-start(f32[1792]{0:T(1024)S(1)} %get-tuple-element.122) | copy-start | bytes 21508 | tf_op jit(solution)/shard_map/cond
  82.8 7.2 %copy-start.4 = (f32[1792]{0:T(1024)S(1)}, f32[1792]{0:T(1024)}, u32[]{:S(2)}) copy-start(f32[1792]{0:T(1024)} %copy-done.3) | copy-start | bytes 21508 | tf_op jit(solution)/shard_map/cond
  96.4 2.2 copy-start.10
  98.6 3.9 %copy-start.5 = (f32[1792]{0:T(1024)}, f32[1792]{0:T(1024)S(1)}, u32[]{:S(2)}) copy-start(f32[1792]{0:T(1024)S(1)} %get-tuple-element.126) | copy-start | bytes 21508 | tf_op jit(solution)/shard_map/cond
  109.0 8.2 %copy-start.6 = (f32[1792]{0:T(1024)S(1)}, f32[1792]{0:T(1024)}, u32[]{:S(2)}) copy-start(f32[1792]{0:T(1024)} %copy-done.5) | copy-start | bytes 21508 | tf_op jit(solution)/shard_map/cond
  180.1 183.9 %reduce-scatter.5.cloned.1.call-start = ((), (), s32[]{:S(2)}) async-start(), calls=%async_computation.2 | async-start | bytes 3096576 | tf_op jit(solution)/shard_map/reduce_scatter | solution.py:138
  183.4 34.4 %copy-start.15 = (s32[8]{0:T(128)S(1)}, s32[8]{0:T(128)}, u32[]{:S(2)}) copy-start(s32[8]{0:T(128)} %param.28) | copy-start | bytes 100
  183.4 37.0 %copy-start.13 = (bf16[1,128]{1,0:T(2,128)(2,1)S(1)}, bf16[1,128]{1,0:T(2,128)(2,1)}, u32[]{:S(2)}) copy-start(bf16[1,128]{1,0:T(2,128)(2,1)} %param.23) | copy-start | bytes 772
  183.4 53.8 %copy-start.14 = (bf16[1,128]{1,0:T(2,128)(2,1)S(1)}, bf16[1,128]{1,0:T(2,128)(2,1)}, u32[]{:S(2)}) copy-start(bf16[1,128]{1,0:T(2,128)(2,1)} %param.24) | copy-start | bytes 772
  183.4 72.0 %copy-start.12 = (bf16[1,896]{1,0:T(2,128)(2,1)S(1)}, bf16[1,896]{1,0:T(2,128)(2,1)}, u32[]{:S(2)}) copy-start(bf16[1,896]{1,0:T(2,128)(2,1)} %param.22) | copy-start | bytes 5380
  183.4 102.7 %copy-start.16 = (bf16[1,4096,128]{2,1,0:T(8,128)(2,1)S(1)}, bf16[1,4096,128]{2,1,0:T(8,128)(2,1)}, u32[]{:S(2)}) copy-start(bf16[1,4096,128]{2,1,0:T(8,128)(2,1)} %param.25) | copy-start | bytes 3145732
  217.1 102.7 %copy-start.17 = (u32[32]{0:T(128)S(1)}, u32[32]{0:T(128)}, u32[]{:S(2)}) copy-start(u32[32]{0:T(128)} %constant.195) | copy-start | bytes 388
  217.4 113.8 %copy-start.9 = (bf16[3,32,128]{2,1,0:T(8,128)(2,1)S(1)}, bf16[3,32,128]{2,1,0:T(8,128)(2,1)}, u32[]{:S(2)}) copy-start(bf16[3,32,128]{2,1,0:T(8,128)(2,1)} %param.32) | copy-start | bytes 73732
  (3 other events, 4.3 us)
Sparse Core Ops, SparseCore 0:
  180.2 58.4 reduce-scatter.6
  242.3 70.6 reduce-scatter.4
